TPU v7x, 256 devices: a whole 4x4x8 slice. The times are simulated.
256 devices in a mesh: grp: 4 (over y), mdl: 64 (over z, x, core).
Axes of the slice: x: 4, y: 4, z: 8, core: 2. Of those that a mesh axis runs over, the one named last changes fastest.
Arguments:
- pol_hidden: bfloat16 [1024, 4096], P(('grp', 'mdl')), may hold values from -6 to 6
- ref_hidden: bfloat16 [1024, 4096], P(('grp', 'mdl')), may hold values from -6 to 6
- pol_mlp_gain: bfloat16 [4096], replicated, may hold values from 0.099609375 to 1.8984375
- ref_mlp_gain: bfloat16 [4096], replicated, may hold values from 0.099609375 to 1.8984375
- pol_final_gain: bfloat16 [4096], replicated, may hold values from 0.099609375 to 1.8984375
- ref_final_gain: bfloat16 [4096], replicated, may hold values from 0.099609375 to 1.8984375
- pol_gate: bfloat16 [4096, 11008], P(None, 'mdl'), may hold values from -0.09375 to 0.09375
- pol_up: bfloat16 [4096, 11008], P(None, 'mdl'), may hold values from -0.09375 to 0.09375
- pol_down: bfloat16 [11008, 4096], P('mdl'), may hold values from -0.109375 to 0.109375
- ref_gate: bfloat16 [4096, 11008], P(None, 'mdl'), may hold values from -0.09375 to 0.09375
- ref_up: bfloat16 [4096, 11008], P(None, 'mdl'), may hold values from -0.09375 to 0.09375
- ref_down: bfloat16 [11008, 4096], P('mdl'), may hold values from -0.109375 to 0.109375
- pol_head: bfloat16 [64000, 4096], P(('grp', 'mdl')), may hold values from -20 to 20
- ref_head: bfloat16 [64000, 4096], P(('grp', 'mdl')), may hold values from -20 to 20
- token_ids: int32 [1024], replicated, may hold values from 0 to 63999
- lengths: int32 [16], replicated, may hold values from 1 to 160, 1024 in all
Outputs:
- pol_out: bfloat16 [1024, 4096], P(('grp', 'mdl'))
- ref_out: bfloat16 [1024, 4096], P(('grp', 'mdl'))
- rollout_ratio: float32 [16], replicated
Inputs may be any that keep to these rules, and one draw needn't show every extreme that they name: Rollout lengths sum to 1024; the longest is exactly 160.
All inputs are finite; a program needn't handle non-finite values.
Results may differ from a plain program's by a relative error of at most 0.012.
The roundings to bfloat16 on the way count: a program that leaves them out, or rounds other values in their place, can miss the bound.
Values may be sent and summed in bfloat16 or wider, within the bound.
No kernel may reach another device: no remote copies, remote signals or barrier semaphores. Data moves between devices by JAX's collectives and lax.ppermute only.
A program may use at most 128 MiB of HBM per device.

v0:
```python
import jax
import jax.numpy as jnp
from jax import lax
from jax.sharding import PartitionSpec as P


def rms_rows(rows, gain):
    values = rows.astype(jnp.float32)
    scale = lax.rsqrt(jnp.mean(values * values, axis=-1, keepdims=True) + 1e-05)
    return (values * scale * gain.astype(jnp.float32)).astype(jnp.bfloat16)


def mlp_partial(piece, gain, w_gate, w_up, w_down):
    normed = rms_rows(piece, gain)
    gate = jnp.dot(normed, w_gate, preferred_element_type=jnp.float32)
    upper = jnp.dot(normed, w_up, preferred_element_type=jnp.float32)
    hidden = (jax.nn.silu(gate) * upper).astype(jnp.bfloat16)
    return jnp.dot(hidden, w_down, preferred_element_type=jnp.float32)


def vocab_terms(token_rows, head_rows, targets, vocab):
    logits = jnp.einsum("td,vd->tv", token_rows, head_rows, preferred_element_type=jnp.float32)
    peak = jnp.max(logits, axis=1)
    total = jnp.sum(jnp.exp(logits - peak[:, None]), axis=1)
    target = jnp.sum(jnp.where(targets[:, None] == vocab[None, :], logits, 0.0), axis=1)
    return (peak, total, target)


def rollout_totals(log_ratio, positions, lengths):
    ends = jnp.cumsum(lengths)
    owner = jnp.sum((positions[:, None] >= ends[None, :]).astype(jnp.int32), axis=1)
    onehot = (owner[:, None] == jnp.arange(lengths.shape[0], dtype=jnp.int32)[None, :]).astype(
        jnp.float32
    )
    return jnp.sum(log_ratio[:, None] * onehot, axis=0)


def per_device(
    pol_hidden,
    ref_hidden,
    pol_mlp_gain,
    ref_mlp_gain,
    pol_final_gain,
    ref_final_gain,
    pol_gate,
    pol_up,
    pol_down,
    ref_gate,
    ref_up,
    ref_down,
    pol_head,
    ref_head,
    token_ids,
    lengths,
):
    rows = pol_hidden.shape[0]
    member = lax.axis_index("mdl")
    group = lax.axis_index("grp")
    members = lax.axis_size("mdl")
    both_in = lax.all_gather(jnp.stack([pol_hidden, ref_hidden]), "mdl", axis=1, tiled=True)
    partials = (
        mlp_partial(both_in[0], pol_mlp_gain, pol_gate, pol_up, pol_down),
        mlp_partial(both_in[1], ref_mlp_gain, ref_gate, ref_up, ref_down),
    )
    mixed = lax.psum(partials, "mdl")
    outs = [(both_in[i].astype(jnp.float32) + mixed[i]).astype(jnp.bfloat16) for i in range(2)]
    finals = jnp.stack([rms_rows(outs[0], pol_final_gain), rms_rows(outs[1], ref_final_gain)])
    own = [lax.dynamic_slice_in_dim(o, member * rows, rows, axis=0) for o in outs]
    every = lax.all_gather(finals, "grp", axis=1, tiled=True)
    voc_dev = pol_head.shape[0]
    positions = jnp.arange(every.shape[1], dtype=jnp.int32)
    vocab = (group * members + member) * voc_dev + jnp.arange(voc_dev, dtype=jnp.int32)
    pol_terms = vocab_terms(every[0], pol_head, token_ids, vocab)
    ref_terms = vocab_terms(every[1], ref_head, token_ids, vocab)
    peaks = lax.pmax(lax.pmax((pol_terms[0], ref_terms[0]), "mdl"), "grp")
    sums = lax.psum(
        lax.psum(
            (
                pol_terms[1] * jnp.exp(pol_terms[0] - peaks[0]),
                pol_terms[2],
                ref_terms[1] * jnp.exp(ref_terms[0] - peaks[1]),
                ref_terms[2],
            ),
            "mdl",
        ),
        "grp",
    )
    pol_logp = sums[1] - peaks[0] - jnp.log(sums[0])
    ref_logp = sums[3] - peaks[1] - jnp.log(sums[2])
    rollout_ratio = rollout_totals(pol_logp - ref_logp, positions, lengths)
    return (own[0], own[1], rollout_ratio)


def solution(mesh):
    placed = (
        P(("grp", "mdl"), None),
        P(("grp", "mdl"), None),
        P(),
        P(),
        P(),
        P(),
        P(None, "mdl"),
        P(None, "mdl"),
        P("mdl", None),
        P(None, "mdl"),
        P(None, "mdl"),
        P("mdl", None),
        P(("grp", "mdl"), None),
        P(("grp", "mdl"), None),
        P(),
        P(),
    )
    return jax.shard_map(
        per_device,
        mesh=mesh,
        in_specs=placed,
        out_specs=(P(("grp", "mdl"), None), P(("grp", "mdl"), None), P()),
        check_vma=False,
    )
```

profile of v0, /device:TPU:8, one launch (start us, length us, event | category | flops | bytes accessed | tf_op | source)
XLA Modules:
  0.0 921.6 jit_solution(18328997950964783200)
XLA Ops:
  7.2 1.0 pad_maximum_fusion.1
  9.0 1.3 convert_element_type.62
  11.0 81.7 %all-gather.3.cloned.1.call-done = bf16[2,256,4096]{2,0,1:T(2,128)(2,1)} async-done(((bf16[2,4,4096]{2,0,1:T(2,128)(2,1)}), bf16[2,256,4096]{2,0,1:T(2,128)(2,1)}) %all-gather.3.cloned.1.call-update) | async-done | bytes 4194320 | tf_op jit(solution)/shard_map/all_gather | solution.py:60
  92.7 13.2 %fusion.48 = (bf16[1,256,4096]{2,0,1:T(2,128)(2,1)S(1)}, bf16[1,256,4096]{2,0,1:T(2,128)(2,1)S(1)}) fusion(bf16[2,256,4096]{2,0,1:T(2,128)(2,1)} %all-gather.3.cloned.1.call-done), kind=kLoop, calls=%fused_computation.76 | loop fusion | bytes 8388608 | tf_op jit(solution)/shard_map/slice | solution.py:66
  105.9 6.7 fusion.8
  113.9 1.6 fusion.30
  115.5 6.6 fusion.21
  122.1 3.7 fusion.26
  125.8 6.6 fusion.20
  133.1 201.9 %all-reduce.7.cloned.1.call-done = (f32[256,4096]{1,0:T(8,128)}, f32[256,4096]{1,0:T(8,128)}) async-done(((f32[256,4096]{1,0:T(8,128)}, f32[256,4096]{1,0:T(8,128)}), (f32[256,4096]{1,0:T(8,128)}, f32[256,4096]{1,0:T(8,128)})) %all-reduce.7.cloned.1.call-update) | async-done | bytes 8388624 | tf_op jit(solution)/shard_map/psum | solution.py:65
  335.0 3.8 fusion.2
  339.7 0.8 fusion.5
  342.5 2.3 pad_maximum_fusion
  345.8 1.5 constant_dynamic-slice_fusion.1
  347.3 1.5 constant_dynamic-slice_fusion
  348.8 151.6 %all-gather.5.cloned.1.call-done = bf16[2,1024,4096]{2,1,0:T(8,128)(2,1)} async-done(((bf16[2,256,4096]{2,1,0:T(8,128)(2,1)}), bf16[2,1024,4096]{2,1,0:T(8,128)(2,1)}) %all-gather.5.cloned.1.call-update) | async-done | bytes 16777232 | tf_op jit(solution)/shard_map/all_gather | solution.py:69
  500.4 5.9 fusion.49
  506.3 2.2 copy-done.14
  509.2 3.4 fusion.50
  512.5 131.0 %all-reduce.2 = (f32[1024]{0:T(1024)S(1)}, f32[1024]{0:T(1024)S(1)}) all-reduce(f32[1024]{0:T(1024)S(1)} %get-tuple-element.35, f32[1024]{0:T(1024)S(1)} %get-tuple-element.33), channel_id=1, replica_groups=mesh['grp'=4,'mdl'=64] {'mdl'}, use_global_device_ids=true, to_apply=%region_21.22 | all-reduce | flops 2048 | bytes 16384 | tf_op jit(solution)/shard_map/pmax | solution.py:75
  643.5 8.4 all-reduce.4
  652.0 1.7 fusion.22
  653.7 246.2 %all-reduce = (f32[1024]{0:T(1024)S(1)}, f32[1024]{0:T(1024)S(1)}, f32[1024]{0:T(1024)S(1)}, f32[1024]{0:T(1024)S(1)}) all-reduce(f32[1024]{0:T(1024)S(1)} %exponential_multiply_fusion, f32[1024]{0:T(1024)S(1)} %get-tuple-element.8, f32[1024]{0:T(1024)S(1)} %exponential_multiply_fusion.1, ...), channel_id=1, replica_groups=mesh['grp'=4,'mdl'=64] {'mdl'}, use_global_device_ids=true, to_apply=%region_24.25 | all-reduce | flops 4096 | bytes 32768 | tf_op jit(solution)/shard_map/psum | solution.py:77
  899.9 14.6 %all-reduce.3 = (f32[1024]{0:T(1024)S(1)}, f32[1024]{0:T(1024)S(1)}, f32[1024]{0:T(1024)S(1)}, f32[1024]{0:T(1024)S(1)}) all-reduce(f32[1024]{0:T(1024)S(1)} %get-tuple-element.9, f32[1024]{0:T(1024)S(1)} %get-tuple-element.10, f32[1024]{0:T(1024)S(1)} %get-tuple-element.11, ...), channel_id=1, replica_groups=mesh['grp'=4,'mdl'=64] {'grp'}, use_global_device_ids=true, to_apply=%region_25.26 | all-reduce | flops 4096 | bytes 32768 | tf_op jit(solution)/shard_map/psum | solution.py:76
  (58 shorter events, 8.5 us)
Async XLA Ops:
  7.2 493.2 %copy-start = (bf16[250,4096]{1,0:T(8,128)(2,1)S(1)}, bf16[250,4096]{1,0:T(8,128)(2,1)}, u32[]{:S(2)}) copy-start(bf16[250,4096]{1,0:T(8,128)(2,1)} %param.28) | copy-start | bytes 6144004
  7.2 85.5 %all-gather.3.cloned.1.call-start = ((), (), s32[]{:S(2)}) async-start(), calls=%async_computation | async-start | bytes 4259840 | tf_op jit(solution)/shard_map/all_gather | solution.py:60
  8.9 326.1 %all-reduce.7.cloned.1.call-start = ((), (), s32[]{:S(2)}) async-start(), calls=%async_computation.2 | async-start | bytes 16777216 | tf_op jit(solution)/shard_map/psum | solution.py:65
  105.9 8.0 copy-start.8
  105.9 8.0 copy-start.16
  112.6 1.3 copy-start.2
  112.6 1.3 copy-start.12
  113.9 1.6 copy-start.6
  122.1 3.7 copy-start.7
  132.4 0.7 copy-start.9
  132.4 0.7 copy-start.10
  132.4 368.0 %all-gather.5.cloned.1.call-start = ((), (), s32[]{:S(2)}) async-start(), calls=%async_computation.1 | async-start | bytes 20971520 | tf_op jit(solution)/shard_map/all_gather | solution.py:69
  335.0 3.9 copy-start.1
  335.0 4.7 copy-start.5
  338.9 3.0 copy-start.3
  340.6 1.3 copy-start.4
  344.8 0.7 copy-start.13
  500.4 8.2 copy-start.14
  500.4 8.7 copy-start.15
  509.2 142.8 %copy-start.11 = (s32[1024]{0:T(1024)S(1)}, s32[1024]{0:T(1024)}, u32[]{:S(2)}) copy-start(s32[1024]{0:T(1024)} %param.30) | copy-start | bytes 12292
Sparse Core Ops, SparseCore 0:
  10.8 81.8 all-gather.2
  132.5 202.4 all-reduce.6
  345.0 155.3 all-gather.4
where the time goes:
time: 922 us
  waiting for transfers between devices  435 us (47%)
  blocking collectives  400 us (43%)
  matrix products  27.8 us (3%)
  local copies, waits for them, and re-layouts  23 us (2%)
  other arithmetic  21.2 us (2%)
  between operations  13.9 us (2%)
    psum x1, blocking collectives, per_device(): lax.psum((pol_terms[1] * jnp.exp(pol_terms[0] - peaks[0]), pol_terms[2],...  246 us
    psum x1, waiting for transfers between devices, per_device(): mixed = lax.psum(partials, 'mdl')  202 us
    all_gather x1, waiting for transfers between devices, per_device(): every = lax.all_gather(finals, 'grp', axis=1, tiled=True)  152 us
    pmax x2, blocking collectives, per_device(): peaks = lax.pmax(lax.pmax((pol_terms[0], ref_terms[0]), 'mdl'), 'grp')  139 us
    all_gather x1, waiting for transfers between devices, per_device(): lax.all_gather(jnp.stack([pol_hidden, ref_hidden]), 'mdl', axis=1, tiled=...  81.7 us
  transfers between devices with their start and end apart: 3, of which 3 were waited for; matrix products, arithmetic and copies ran while one was open for 1% of the time, Pallas kernels for 0%

commit v1 on v0

--- a/solution.py
+++ b/solution.py
@@ -57,7 +57,16 @@
     member = lax.axis_index("mdl")
     group = lax.axis_index("grp")
     members = lax.axis_size("mdl")
-    both_in = lax.all_gather(jnp.stack([pol_hidden, ref_hidden]), "mdl", axis=1, tiled=True)
+    s0 = jnp.stack([pol_hidden, ref_hidden])
+    both_in = jnp.concatenate(
+        lax.all_to_all(
+            jnp.stack([s0] * lax.psum(1, axis_name="mdl")),
+            axis_name="mdl",
+            split_axis=0,
+            concat_axis=0,
+        ),
+        axis=1,
+    )
     partials = (
         mlp_partial(both_in[0], pol_mlp_gain, pol_gate, pol_up, pol_down),
         mlp_partial(both_in[1], ref_mlp_gain, ref_gate, ref_up, ref_down),

time: 922 us -> 957 us (1.038)
  waiting for transfers between devices: 435 us -> 448 us
  starting transfers between devices: 0.3 us -> 12.6 us
    all_to_all x0 -> x1, waiting for transfers between devices: none -> 95.6 us  [per_device(): lax.all_to_all(jnp.stack([s0] * lax.psum(1, axis_name='mdl')), axis_name=...]
    all_gather x1 -> x0, waiting for transfers between devices: 81.7 us -> none  [per_device(): lax.all_gather(jnp.stack([pol_hidden, ref_hidden]), 'mdl', axis=1, tiled=...]
    slice x1 -> x0, local copies, waits for them, and re-layouts: 13.2 us -> none  [per_device(): both_in[i].astype(jnp.float32) + mixed[i]]
    all_to_all x0 -> x1, starting transfers between devices: none -> 12.3 us  [per_device(): lax.all_to_all(jnp.stack([s0] * lax.psum(1, axis_name='mdl')), axis_name=...]
    convert_element_type x0 -> x2, local copies, waits for them, and re-layouts: none -> 10.6 us  [per_device(): both_in[i].astype(jnp.float32) + mixed[i]]
  transfers between devices with their start and end apart: 3 -> 3, of which waited for: 3 -> 3; matrix products, arithmetic and copies ran while one was open for 1% -> 0% of each run, Pallas kernels for 0% -> 0%
where the time goes in v1:
time: 957 us; the launch traced here: 956 us
  waiting for transfers between devices  448 us (47%)
  blocking collectives  400 us (42%)
  matrix products  32.5 us (3%)
  local copies, waits for them, and re-layouts  25.3 us (3%)
  other arithmetic  23.5 us (2%)
  between operations  14.2 us (1%)
  starting transfers between devices  12.6 us (1%)
    psum x1, blocking collectives, per_device(): lax.psum((pol_terms[1] * jnp.exp(pol_terms[0] - peaks[0]), pol_terms[2],...  246 us
    psum x1, waiting for transfers between devices, per_device(): mixed = lax.psum(partials, 'mdl')  201 us
    all_gather x1, waiting for transfers between devices, per_device(): every = lax.all_gather(finals, 'grp', axis=1, tiled=True)  152 us
    pmax x2, blocking collectives, per_device(): peaks = lax.pmax(lax.pmax((pol_terms[0], ref_terms[0]), 'mdl'), 'grp')  139 us
    all_to_all x1, waiting for transfers between devices, per_device(): lax.all_to_all(jnp.stack([s0] * lax.psum(1, axis_name='mdl')), axis_name=...  95.6 us
  transfers between devices with their start and end apart: 3, of which 3 were waited for; matrix products, arithmetic and copies ran while one was open for 0% of the time, Pallas kernels for 0%

profile of v1, /device:TPU:8, one launch (start us, length us, event | category | flops | bytes accessed | tf_op | source)
XLA Modules:
  0.0 956.4 jit_solution(10177503376572032478)
XLA Ops:
  8.2 4.1 stack.17
  12.2 12.3 %all-to-all-start = ((bf16[64,2,4,4096]{3,2,1,0:T(4,128)(2,1)}), bf16[64,2,4,4096]{3,2,1,0:T(4,128)(2,1)}, u32[]{:S(2)}, u32[]{:S(2)}) async-start(bf16[64,2,4,4096]{3,2,1,0:T(4,128)(2,1)} %stack.17), calls=%async_computation | async-start | bytes 8388608 | tf_op jit(solution)/shard_map/all_to_all | solution.py:62
  25.2 95.6 %all-to-all-done = bf16[64,2,4,4096]{3,2,1,0:T(4,128)(2,1)} async-done(((bf16[64,2,4,4096]{3,2,1,0:T(4,128)(2,1)}), bf16[64,2,4,4096]{3,2,1,0:T(4,128)(2,1)}, u32[]{:S(2)}, u32[]{:S(2)}) %all-to-all-start) | async-done | bytes 4194336 | tf_op jit(solution)/shard_map/all_to_all | solution.py:62
  120.8 3.9 multiply_reduce_fusion
  124.7 6.8 slice_convert_fusion
  132.1 5.3 reshape.111
  138.0 5.3 reshape.110
  143.3 4.4 fusion.31
  147.7 7.2 fusion.12
  154.9 4.4 fusion.30
  159.3 7.2 fusion.13
  167.2 201.0 %all-reduce.7.cloned.1.call-done = (f32[256,4096]{1,0:T(8,128)}, f32[256,4096]{1,0:T(8,128)}) async-done(((f32[256,4096]{1,0:T(8,128)}, f32[256,4096]{1,0:T(8,128)}), (f32[256,4096]{1,0:T(8,128)}, f32[256,4096]{1,0:T(8,128)})) %all-reduce.7.cloned.1.call-update) | async-done | bytes 8388624 | tf_op jit(solution)/shard_map/psum | solution.py:74
  368.3 4.3 fusion.2
  372.9 2.0 copy-done.4
  377.0 2.3 pad_maximum_fusion
  383.2 151.6 %all-gather.2.cloned.1.call-done = bf16[2,1024,4096]{2,1,0:T(8,128)(2,1)} async-done(((bf16[2,256,4096]{2,1,0:T(8,128)(2,1)}), bf16[2,1024,4096]{2,1,0:T(8,128)(2,1)}) %all-gather.2.cloned.1.call-update) | async-done | bytes 16777232 | tf_op jit(solution)/shard_map/all_gather | solution.py:78
  534.9 5.9 fusion.32
  540.8 2.2 copy-done.13
  543.6 3.4 fusion.33
  547.0 131.0 %all-reduce.2 = (f32[1024]{0:T(1024)S(1)}, f32[1024]{0:T(1024)S(1)}) all-reduce(f32[1024]{0:T(1024)S(1)} %get-tuple-element.33, f32[1024]{0:T(1024)S(1)} %get-tuple-element.31), channel_id=1, replica_groups=mesh['grp'=4,'mdl'=64] {'mdl'}, use_global_device_ids=true, to_apply=%region_21.22 | all-reduce | flops 2048 | bytes 16384 | tf_op jit(solution)/shard_map/pmax | solution.py:84
  678.0 8.4 all-reduce.4
  686.4 1.7 fusion.14
  688.2 246.2 %all-reduce = (f32[1024]{0:T(1024)S(1)}, f32[1024]{0:T(1024)S(1)}, f32[1024]{0:T(1024)S(1)}, f32[1024]{0:T(1024)S(1)}) all-reduce(f32[1024]{0:T(1024)S(1)} %exponential_multiply_fusion, f32[1024]{0:T(1024)S(1)} %get-tuple-element.10, f32[1024]{0:T(1024)S(1)} %exponential_multiply_fusion.1, ...), channel_id=1, replica_groups=mesh['grp'=4,'mdl'=64] {'mdl'}, use_global_device_ids=true, to_apply=%region_24.25 | all-reduce | flops 4096 | bytes 32768 | tf_op jit(solution)/shard_map/psum | solution.py:86
  934.3 14.6 %all-reduce.3 = (f32[1024]{0:T(1024)S(1)}, f32[1024]{0:T(1024)S(1)}, f32[1024]{0:T(1024)S(1)}, f32[1024]{0:T(1024)S(1)}) all-reduce(f32[1024]{0:T(1024)S(1)} %get-tuple-element.11, f32[1024]{0:T(1024)S(1)} %get-tuple-element.12, f32[1024]{0:T(1024)S(1)} %get-tuple-element.13, ...), channel_id=1, replica_groups=mesh['grp'=4,'mdl'=64] {'grp'}, use_global_device_ids=true, to_apply=%region_25.26 | all-reduce | flops 4096 | bytes 32768 | tf_op jit(solution)/shard_map/psum | solution.py:85
  (56 shorter events, 11.2 us)
Async XLA Ops:
  7.2 527.7 %copy-start = (bf16[250,4096]{1,0:T(8,128)(2,1)S(1)}, bf16[250,4096]{1,0:T(8,128)(2,1)}, u32[]{:S(2)}) copy-start(bf16[250,4096]{1,0:T(8,128)(2,1)} %param.28) | copy-start | bytes 6144004
  12.2 12.4 %copy-start.7 = (bf16[4096]{0:T(1024)(128)(2,1)S(1)}, bf16[4096]{0:T(1024)(128)(2,1)}, u32[]{:S(2)}) copy-start(bf16[4096]{0:T(1024)(128)(2,1)} %param.19) | copy-start | bytes 24580
  12.2 13.0 %copy-start.8 = (bf16[4096]{0:T(1024)(128)(2,1)S(1)}, bf16[4096]{0:T(1024)(128)(2,1)}, u32[]{:S(2)}) copy-start(bf16[4096]{0:T(1024)(128)(2,1)} %param.18) | copy-start | bytes 24580
  12.2 108.6 %all-to-all-start = ((bf16[64,2,4,4096]{3,2,1,0:T(4,128)(2,1)}), bf16[64,2,4,4096]{3,2,1,0:T(4,128)(2,1)}, u32[]{:S(2)}, u32[]{:S(2)}) async-start(bf16[64,2,4,4096]{3,2,1,0:T(4,128)(2,1)} %stack.17), calls=%async_computation | async-start | bytes 8388608 | tf_op jit(solution)/shard_map/all_to_all | solution.py:62
  24.6 343.7 %all-reduce.7.cloned.1.call-start = ((), (), s32[]{:S(2)}) async-start(), calls=%async_computation.2 | async-start | bytes 16777216 | tf_op jit(solution)/shard_map/psum | solution.py:74
  143.3 4.4 copy-start.5
  154.9 4.4 copy-start.6
  166.5 0.7 copy-start.9
  166.5 0.7 copy-start.10
  166.6 368.3 %all-gather.2.cloned.1.call-start = ((), (), s32[]{:S(2)}) async-start(), calls=%async_computation.1 | async-start | bytes 20971520 | tf_op jit(solution)/shard_map/all_gather | solution.py:78
  368.3 4.6 copy-start.1
  368.3 6.7 copy-start.4
  372.6 3.1 copy-start.2
  375.7 1.4 copy-start.3
  379.3 0.7 copy-start.12
  534.9 8.2 copy-start.13
  534.9 8.7 copy-start.14
  543.6 142.8 %copy-start.11 = (s32[1024]{0:T(1024)S(1)}, s32[1024]{0:T(1024)}, u32[]{:S(2)}) copy-start(s32[1024]{0:T(1024)} %param.30) | copy-start | bytes 12292
Sparse Core Ops, SparseCore 0:
  166.7 201.5 all-reduce.6
  379.4 155.3 all-gather.1
